TPU v7x, 256 devices: a whole 4x4x8 slice. The times are simulated.
256 devices in a mesh: query: 8 (over x, core), bank: 32 (over z, y).
Axes of the slice: x: 4, y: 4, z: 8, core: 2. Of those that a mesh axis runs over, the one named last changes fastest.
Arguments:
- queries: bfloat16 [2048, 32, 128], P(('query', 'bank'))
- passages: bfloat16 [8192, 128, 128], P('bank')
- passage_home: int32 [8192], replicated, may hold values from 0 to 8191, as said below
- candidates: int32 [2048, 16], P(('query', 'bank')), may hold values from 0 to 8191, as said below
- positive: int32 [2048], P(('query', 'bank')), may hold values from 0 to 15
Outputs:
- losses: float32 [2048], P(('query', 'bank'))
- query_grads: float32 [2048, 32, 128], P(('query', 'bank'))
Inputs may be any that keep to these rules, and one draw needn't show every extreme that they name: `passage_home`: each passage id has its own storage row; storage row r lies on bank index r // 256. `candidates`: among the 128 list entries of one device's queries (aligned blocks of 8 queries, in order), at most 12 name passages stored on one bank index; in every block some bank index gets exactly 12, and in each group of 32 consecutive blocks it is the same bank index for all of them.
All inputs are finite; a program needn't handle non-finite values.
Results may differ from a plain program's by a relative error of at most 0.0049.
Values may be sent and summed in bfloat16 or wider, within the bound.
No kernel may reach another device: no remote copies, remote signals or barrier semaphores. Data moves between devices by JAX's collectives and lax.ppermute only.
A program may use at most 128 MiB of HBM per device.

v0:
```python
import jax
import jax.numpy as jnp
from jax import lax
from jax.sharding import PartitionSpec as P


def soft_terms(scores):
    largest = jnp.max(scores, axis=-1, keepdims=True)
    raised = jnp.exp(scores - largest)
    totals = jnp.sum(raised, axis=-1, keepdims=True)
    maxima = largest[..., 0] + jnp.log(totals[..., 0])
    weights = (raised / totals).astype(jnp.bfloat16)
    return (maxima, weights)


def contrast(similarity, positive):
    largest = jnp.max(similarity, axis=1, keepdims=True)
    raised = jnp.exp(similarity - largest)
    totals = jnp.sum(raised, axis=1, keepdims=True)
    picked = jnp.arange(similarity.shape[1], dtype=jnp.int32)[None, :] == positive[:, None]
    losses = (
        largest[:, 0] + jnp.log(totals[:, 0]) - jnp.sum(jnp.where(picked, similarity, 0.0), axis=1)
    )
    coefficients = (raised / totals - picked.astype(jnp.float32)).astype(jnp.bfloat16)
    return (losses, coefficients)


def body(queries, passages, passage_home, candidates, positive):
    shards = lax.axis_size("bank")
    me = lax.axis_index("bank")
    query_rows, query_len, feature_dim = queries.shape
    listed = candidates.shape[1]
    holdings = passages.shape[0]
    tile_len = passages.shape[1]
    entries = query_rows * listed
    capacity = 3 * entries // shards
    group_rows = shards * query_rows
    lists = jnp.concatenate([candidates, positive[:, None]], axis=1)
    lists = lax.all_gather(lists, "bank", axis=0, tiled=True)
    group_candidates = lists[:, :listed]
    group_positive = lists[:, listed]
    group_queries = lax.all_gather(queries, "bank", axis=0, tiled=True)
    storage = passage_home[group_candidates].reshape(shards, entries)
    mine = storage // holdings == me
    position = jnp.cumsum(mine.astype(jnp.int32), axis=1) - 1
    slot_ids = jnp.arange(capacity, dtype=jnp.int32)
    hit = mine[:, None, :] & (position[:, None, :] == slot_ids[None, :, None])
    valid = jnp.any(hit, axis=2)
    entry_ids = jnp.arange(entries, dtype=jnp.int32)
    entry = jnp.sum(jnp.where(hit, entry_ids[None, None, :], 0), axis=2)
    local_slot = jnp.sum(jnp.where(hit, (storage % holdings)[:, None, :], 0), axis=2)
    source = jnp.arange(shards, dtype=jnp.int32)[:, None]
    query_index = (source * query_rows + entry // listed).reshape(-1)
    flat_index = (source * entries + entry).reshape(-1)
    valid = valid.reshape(-1)
    local_slot = local_slot.reshape(-1)
    passage_tiles = passages[local_slot]
    query_tiles = group_queries[query_index]
    scores = jnp.einsum(
        "sid,sjd->sij", query_tiles, passage_tiles, preferred_element_type=jnp.float32
    )
    maxima, weights = soft_terms(scores)
    token_basis = jnp.einsum(
        "sij,sjd->sid", weights, passage_tiles, preferred_element_type=jnp.float32
    ).astype(jnp.bfloat16)
    slot_similarity = jnp.sum(maxima, axis=1)
    place = flat_index[:, None] == jnp.arange(group_rows * listed, dtype=jnp.int32)[None, :]
    place = place & valid[:, None]
    similarity = jnp.sum(jnp.where(place, slot_similarity[:, None], 0.0), axis=0)
    similarity = lax.psum(similarity, "bank").reshape(group_rows, listed)
    losses, coefficients = contrast(similarity, group_positive)
    slot_coefficient = jnp.where(
        valid, coefficients.reshape(-1)[flat_index], jnp.zeros((), jnp.bfloat16)
    )
    owner = query_index[:, None] == jnp.arange(group_rows, dtype=jnp.int32)[None, :]
    spread = jnp.where(owner, slot_coefficient[:, None], jnp.zeros((), jnp.bfloat16))
    partial = jnp.einsum(
        "sq,sd->qd",
        spread,
        token_basis.reshape(-1, query_len * feature_dim),
        preferred_element_type=jnp.float32,
    )
    gradient = lax.psum_scatter(partial, "bank", scatter_dimension=0, tiled=True)
    own_losses = lax.dynamic_slice_in_dim(losses, me * query_rows, query_rows)
    return (own_losses, gradient.reshape(query_rows, query_len, feature_dim))


def solution(mesh):
    return jax.shard_map(
        body,
        mesh=mesh,
        in_specs=(
            P(("query", "bank"), None, None),
            P("bank", None, None),
            P(),
            P(("query", "bank"), None),
            P(("query", "bank")),
        ),
        out_specs=(P(("query", "bank")), P(("query", "bank"), None, None)),
        check_vma=False,
    )
```

profile of v0, /device:TPU:4, one launch (start us, length us, event | category | flops | bytes accessed | tf_op | source)
XLA Modules:
  0.0 502.4 jit_solution(9782047059398808998)
XLA Ops:
  7.2 0.0 all-gather.2.cloned.1.call-start
  7.2 0.7 all-gather.2.cloned.1.call-update
  7.9 0.0 reduce-scatter.2.cloned.1.call-start
  8.0 0.7 copy.13
  8.7 0.8 pad_add_fusion
  9.5 46.7 %all_gather.6 = s32[256,17]{1,0:T(8,128)S(1)} all-gather(s32[8,17]{1,0:T(8,128)S(1)} %pad_add_fusion), channel_id=1, replica_groups=mesh['query'=8,'bank'=32] {'bank'}, dimensions={0}, use_global_device_ids=true | all-gather | bytes 17952 | tf_op jit(solution)/shard_map/all_gather | solution.py:39
  56.2 0.1 reshape.316
  56.3 23.0 %gather_fusion = s32[4096]{0:T(1024)S(1)} fusion(s32[8192]{0:T(1024)S(1)} %copy-done, s32[4096]{0:T(1024)S(1)} %broadcast_clamp_fusion), kind=kCustom, calls=%fused_computation | custom fusion | bytes 49152 | tf_op jit(solution)/shard_map/gather | solution.py:43
  79.4 0.3 reduce_window_sum.11
  79.7 0.5 select_reduce_fusion.1
  80.2 0.1 copy.14
  80.3 0.1 reduce_sum.69
  80.4 0.1 reduce_sum.68
  80.5 0.1 add.142
  80.6 0.1 add.158
  80.7 0.1 add.143
  80.8 0.1 add.147
  80.9 0.1 add.148
  81.0 0.1 add.156
  81.1 0.1 copy.17
  81.2 0.1 reshape.309
  81.3 0.3 fusion.13
  81.6 0.1 copy.15
  81.7 0.1 and.84
  81.8 0.2 slice_reduce_fusion
  82.0 0.1 fusion.14
  82.1 0.1 reshape.313
  82.2 14.4 %gather_fusion.2 = bf16[384,128,128]{2,1,0:T(8,128)(2,1)} fusion(bf16[256,128,128]{2,1,0:T(8,128)(2,1)} %param.6, s32[1024]{0:T(1024)S(1)} %pad_clamp_fusion.1), kind=kCustom, calls=%fused_computation.2 | custom fusion | bytes 25167360 | tf_op jit(solution)/shard_map/gather | solution.py:57
  96.7 0.0 all-gather.2.cloned.1.call-done
  96.7 2.8 gather_fusion.1
  99.6 11.3 %fusion.30 = (f32[384,32]{1,0:T(8,128)S(1)}, f32[384,32,128]{2,1,0:T(8,128)}) fusion(bf16[384,32,128]{2,1,0:T(8,128)(2,1)S(1)} %gather_fusion.1, bf16[384,128,128]{2,1,0:T(8,128)(2,1)} %gather_fusion.2), kind=kOutput, calls=%fused_computation.76 | convolution fusion | flops 404213760 | bytes 22069248 | tf_op jit(solution)/shard_map/sid,sjd->sij/dot_general | solution.py:59
  110.9 5.8 %fusion.1 = f32[384,32]{1,0:T(8,128)S(1)} fusion(f32[384,32,128]{2,1,0:T(8,128)} %get-tuple-element.21, f32[384,32]{1,0:T(8,128)S(1)} %get-tuple-element.20), kind=kLoop, calls=%fused_computation.9 | loop fusion | flops 3133440 | bytes 6389760 | tf_op jit(solution)/shard_map/reduce_sum | solution.py:10
  116.8 0.2 add_reduce_fusion
  116.9 7.1 %fusion.8 = bf16[384,32,128]{2,1,0:T(8,128)(2,1)S(1)} fusion(bf16[384,128,128]{2,1,0:T(8,128)(2,1)} %gather_fusion.2, f32[384,32,128]{2,1,0:T(8,128)S(1)} %copy-done.1, f32[384,32]{1,0:T(8,128)S(1)} %fusion.1, f32[384,32]{1,0:T(8,128)S(1)} %get-tuple-element.20), kind=kOutput, calls=%fused_computation.16 | convolution fusion | flops 408944640 | bytes 22118400 | tf_op jit(solution)/shard_map/sij,sjd->sid/dot_general | solution.py:63
  124.1 1.9 select_reduce_fusion
  126.0 140.5 %psum.7 = f32[4096]{0:T(1024)S(1)} all-reduce(f32[4096]{0:T(1024)S(1)} %select_reduce_fusion), channel_id=1, replica_groups=mesh['query'=8,'bank'=32] {'bank'}, use_global_device_ids=true, to_apply=%region_8.9 | all-reduce | flops 4096 | bytes 32768 | tf_op jit(solution)/shard_map/psum | solution.py:70
  266.5 0.1 reshape.310
  266.6 0.1 reduce_max.19
  266.7 0.3 exponential_reduce_fusion
  267.0 0.1 div.63
  267.1 0.1 div.64
  267.2 0.1 sub.51
  267.3 0.1 sub.55
  267.4 2.8 gather_fusion.3
  270.2 3.4 fusion.3
  273.7 0.6 dynamic_slice.3
  274.3 219.7 %reduce-scatter.2.cloned.1.call-done = f32[8,4096]{1,0:T(8,128)} async-done(((f32[256,4096]{1,0:T(8,128)}), f32[8,4096]{1,0:T(8,128)}) %reduce-scatter.2.cloned.1.call-update) | async-done | bytes 131088 | tf_op jit(solution)/shard_map/reduce_scatter | solution.py:83
  494.0 1.6 copy.18
  (20 shorter events, 0.2 us)
Async XLA Ops:
  7.2 49.1 %copy-start = (s32[8192]{0:T(1024)S(1)}, s32[8192]{0:T(1024)}, u32[]{:S(2)}) copy-start(s32[8192]{0:T(1024)} %param.7) | copy-start | bytes 98308
  7.2 89.6 %all-gather.2.cloned.1.call-start = ((), (), s32[]{:S(2)}) async-start(), calls=%async_computation.1 | async-start | bytes 2162688 | tf_op jit(solution)/shard_map/all_gather | solution.py:42
  7.9 486.1 %reduce-scatter.2.cloned.1.call-start = ((), (), s32[]{:S(2)}) async-start(), calls=%async_computation.2 | async-start | bytes 4325376 | tf_op jit(solution)/shard_map/reduce_scatter | solution.py:83
  110.9 6.0 %copy-start.1 = (f32[384,32,128]{2,1,0:T(8,128)S(1)}, f32[384,32,128]{2,1,0:T(8,128)}, u32[]{:S(2)}) copy-start(f32[384,32,128]{2,1,0:T(8,128)} %get-tuple-element.21) | copy-start | bytes 18874372
Sparse Core Ops, SparseCore 0:
  10.6 80.7 all-gather.1
  273.8 220.1 reduce-scatter.1
where the time goes:
time: 503 us; the launch traced here: 502 us
  waiting for transfers between devices  220 us (44%)
  blocking collectives  187 us (37%)
  local copies, waits for them, and re-layouts  48.1 us (10%)
  matrix products  21.9 us (4%)
  between operations  14.3 us (3%)
  other arithmetic  10.4 us (2%)
    reduce_scatter x1, waiting for transfers between devices, body(): lax.psum_scatter(partial, 'bank', scatter_dimension=0, tiled=True)  220 us
    psum x1, blocking collectives, body(): similarity = lax.psum(similarity, 'bank').reshape(group_rows, listed)  141 us
    all_gather x1, blocking collectives, body(): lists = lax.all_gather(lists, 'bank', axis=0, tiled=True)  46.7 us
    gather x1, local copies, waits for them, and re-layouts, body(): storage = passage_home[group_candidates].reshape(shards, entries)  23 us
    gather x1, local copies, waits for them, and re-layouts, body(): passage_tiles = passages[local_slot]  14.4 us
    dot_general x1, matrix products, body(): jnp.einsum('sid,sjd->sij', query_tiles, passage_tiles, preferred_element_...  11.3 us
  transfers between devices with their start and end apart: 2, of which 1 were waited for; matrix products, arithmetic and copies ran while one was open for 8% of the time, Pallas kernels for 0%

commit v1 on v0

--- a/solution.py
+++ b/solution.py
@@ -67,7 +67,10 @@
     place = flat_index[:, None] == jnp.arange(group_rows * listed, dtype=jnp.int32)[None, :]
     place = place & valid[:, None]
     similarity = jnp.sum(jnp.where(place, slot_similarity[:, None], 0.0), axis=0)
-    similarity = lax.psum(similarity, "bank").reshape(group_rows, listed)
+    _put_widths = lambda lane_axis, block_here: lax.all_gather(block_here, axis_name=lane_axis).sum(
+        axis=0
+    )
+    similarity = _put_widths("bank", similarity).reshape(group_rows, listed)
     losses, coefficients = contrast(similarity, group_positive)
     slot_coefficient = jnp.where(
         valid, coefficients.reshape(-1)[flat_index], jnp.zeros((), jnp.bfloat16)

time: 503 us -> 419 us (0.83)
  blocking collectives: 187 us -> 99.7 us
    psum x1 -> x0, blocking collectives: 141 us -> none  [body(): similarity = lax.psum(similarity, 'bank').reshape(group_rows, listed)]
    all_gather x0 -> x1, blocking collectives: none -> 52.9 us  [body(): lax.all_gather(block_here, axis_name=lane_axis).sum(axis=0)]
  transfers between devices with their start and end apart: 2 -> 2, of which waited for: 1 -> 1; matrix products, arithmetic and copies ran while one was open for 8% -> 10% of each run, Pallas kernels for 0% -> 0%
where the time goes in v1:
time: 419 us; the launch traced here: 418 us
  waiting for transfers between devices  221 us (53%)
  blocking collectives  99.7 us (24%)
  local copies, waits for them, and re-layouts  50.1 us (12%)
  matrix products  21.9 us (5%)
  between operations  14.3 us (3%)
  other arithmetic  11.5 us (3%)
    reduce_scatter x1, waiting for transfers between devices, body(): lax.psum_scatter(partial, 'bank', scatter_dimension=0, tiled=True)  220 us
    all_gather x1, blocking collectives, body(): lax.all_gather(block_here, axis_name=lane_axis).sum(axis=0)  52.9 us
    all_gather x1, blocking collectives, body(): lists = lax.all_gather(lists, 'bank', axis=0, tiled=True)  46.7 us
    gather x1, local copies, waits for them, and re-layouts, body(): storage = passage_home[group_candidates].reshape(shards, entries)  23 us
    gather x1, local copies, waits for them, and re-layouts, body(): passage_tiles = passages[local_slot]  14.4 us
    dot_general x1, matrix products, body(): jnp.einsum('sid,sjd->sij', query_tiles, passage_tiles, preferred_element_...  11.3 us
  transfers between devices with their start and end apart: 2, of which 1 were waited for; matrix products, arithmetic and copies ran while one was open for 10% of the time, Pallas kernels for 0%

profile of v1, /device:TPU:4, one launch (start us, length us, event | category | flops | bytes accessed | tf_op | source)
XLA Modules:
  0.0 418.3 jit_solution(3127906398412858952)
XLA Ops:
  7.2 0.7 all-gather.3.cloned.1.call-update
  7.9 0.0 reduce-scatter.2.cloned.1.call-start
  8.0 0.7 copy.13
  8.7 0.8 pad_add_fusion
  9.5 46.7 %all_gather.12 = s32[256,17]{1,0:T(8,128)S(1)} all-gather(s32[8,17]{1,0:T(8,128)S(1)} %pad_add_fusion), channel_id=1, replica_groups=mesh['query'=8,'bank'=32] {'bank'}, dimensions={0}, use_global_device_ids=true | all-gather | bytes 17952 | tf_op jit(solution)/shard_map/all_gather | solution.py:39
  56.2 0.1 reshape.316
  56.3 23.0 %gather_fusion = s32[4096]{0:T(1024)S(1)} fusion(s32[8192]{0:T(1024)S(1)} %copy-done, s32[4096]{0:T(1024)S(1)} %broadcast_clamp_fusion), kind=kCustom, calls=%fused_computation | custom fusion | bytes 49152 | tf_op jit(solution)/shard_map/gather | solution.py:43
  79.4 0.3 reduce_window_sum.11
  79.7 0.5 select_reduce_fusion.1
  80.2 0.1 copy.14
  80.3 0.1 reduce_sum.78
  80.4 0.1 reduce_sum.77
  80.5 0.1 add.140
  80.6 0.1 add.156
  80.7 0.1 add.141
  80.8 0.1 add.145
  80.9 0.1 add.146
  81.0 0.1 add.154
  81.1 0.1 copy.17
  81.2 0.1 reshape.309
  81.3 0.3 fusion.13
  81.6 0.1 copy.15
  81.7 0.1 and.84
  81.8 0.2 slice_reduce_fusion
  82.0 0.1 fusion.14
  82.1 0.1 reshape.313
  82.2 14.4 %gather_fusion.2 = bf16[384,128,128]{2,1,0:T(8,128)(2,1)} fusion(bf16[256,128,128]{2,1,0:T(8,128)(2,1)} %param.6, s32[1024]{0:T(1024)S(1)} %pad_clamp_fusion.1), kind=kCustom, calls=%fused_computation.2 | custom fusion | bytes 25167360 | tf_op jit(solution)/shard_map/gather | solution.py:57
  96.7 2.8 gather_fusion.1
  99.6 11.3 %fusion.30 = (f32[384,32]{1,0:T(8,128)S(1)}, f32[384,32,128]{2,1,0:T(8,128)}) fusion(bf16[384,32,128]{2,1,0:T(8,128)(2,1)S(1)} %gather_fusion.1, bf16[384,128,128]{2,1,0:T(8,128)(2,1)} %gather_fusion.2), kind=kOutput, calls=%fused_computation.76 | convolution fusion | flops 404213760 | bytes 22069248 | tf_op jit(solution)/shard_map/sid,sjd->sij/dot_general | solution.py:59
  110.9 5.8 %fusion.1 = f32[384,32]{1,0:T(8,128)S(1)} fusion(f32[384,32,128]{2,1,0:T(8,128)} %get-tuple-element.21, f32[384,32]{1,0:T(8,128)S(1)} %get-tuple-element.20), kind=kLoop, calls=%fused_computation.9 | loop fusion | flops 3133440 | bytes 6389760 | tf_op jit(solution)/shard_map/reduce_sum | solution.py:10
  116.8 0.2 add_reduce_fusion
  116.9 7.1 %fusion.8 = bf16[384,32,128]{2,1,0:T(8,128)(2,1)S(1)} fusion(bf16[384,128,128]{2,1,0:T(8,128)(2,1)} %gather_fusion.2, f32[384,32,128]{2,1,0:T(8,128)S(1)} %copy-done.1, f32[384,32]{1,0:T(8,128)S(1)} %fusion.1, f32[384,32]{1,0:T(8,128)S(1)} %get-tuple-element.20), kind=kOutput, calls=%fused_computation.16 | convolution fusion | flops 408944640 | bytes 22118400 | tf_op jit(solution)/shard_map/sij,sjd->sid/dot_general | solution.py:63
  124.1 1.9 select_reduce_fusion
  126.0 52.9 %all-gather = f32[131072]{0:T(1024)} all-gather(f32[4096]{0:T(1024)S(1)} %select_reduce_fusion), channel_id=2, replica_groups=mesh['query'=8,'bank'=32] {'bank'}, dimensions={0}, use_global_device_ids=true | all-gather | bytes 540672 | tf_op jit(solution)/shard_map/all_gather | solution.py:70
  178.9 2.0 reshape.346
  180.9 1.1 reduce_sum.83
  182.0 0.1 reshape.310
  182.1 0.1 reduce_max.19
  182.2 0.3 exponential_reduce_fusion
  182.5 0.1 div.63
  182.6 0.1 div.64
  182.7 0.1 sub.51
  182.8 0.1 sub.55
  182.9 2.8 gather_fusion.3
  185.7 3.4 fusion.3
  189.2 0.6 dynamic_slice.3
  189.8 220.1 %reduce-scatter.2.cloned.1.call-done = f32[8,4096]{1,0:T(8,128)} async-done(((f32[256,4096]{1,0:T(8,128)}), f32[8,4096]{1,0:T(8,128)}) %reduce-scatter.2.cloned.1.call-update) | async-done | bytes 131088 | tf_op jit(solution)/shard_map/reduce_scatter | solution.py:86
  409.9 1.6 copy.18
  (22 shorter events, 0.3 us)
Async XLA Ops:
  7.2 49.1 %copy-start = (s32[8192]{0:T(1024)S(1)}, s32[8192]{0:T(1024)}, u32[]{:S(2)}) copy-start(s32[8192]{0:T(1024)} %param.7) | copy-start | bytes 98308
  7.2 89.6 %all-gather.3.cloned.1.call-start = ((), (), s32[]{:S(2)}) async-start(), calls=%async_computation.1 | async-start | bytes 2162688 | tf_op jit(solution)/shard_map/all_gather | solution.py:42
  7.9 402.0 %reduce-scatter.2.cloned.1.call-start = ((), (), s32[]{:S(2)}) async-start(), calls=%async_computation.2 | async-start | bytes 4325376 | tf_op jit(solution)/shard_map/reduce_scatter | solution.py:86
  110.9 6.0 %copy-start.1 = (f32[384,32,128]{2,1,0:T(8,128)S(1)}, f32[384,32,128]{2,1,0:T(8,128)}, u32[]{:S(2)}) copy-start(f32[384,32,128]{2,1,0:T(8,128)} %get-tuple-element.21) | copy-start | bytes 18874372
Sparse Core Ops, SparseCore 0:
  10.6 80.7 all-gather.2
  189.3 220.5 reduce-scatter.1
